TPU v7x, 32 devices: a whole 2x2x4 slice. The times are simulated.
32 devices in a mesh: ctx: 8 (over z, y), tp: 4 (over x, core).
Axes of the slice: x: 2, y: 2, z: 4, core: 2. Of those that a mesh axis runs over, the one named last changes fastest.
Arguments:
- tokens: bfloat16 [6144, 4096], P('ctx'), may hold values from -6 to 6
- in_weight: bfloat16 [4096, 3, 4096], P('ctx', None, 'tp'), may hold values from -0.09375 to 0.09375
- short_taps: float32 [3, 4096, 7], P(None, 'tp'), may hold values from -2.5 to 2.5
- medium_taps: float32 [4096, 128], P('tp'), may hold values from -2 to 2
- medium_decay: float32 [4096], P('tp'), may hold values from 0.01 to 0.3
- skip_gain: float32 [4096], P('tp'), may hold values from 0.5 to 1.5
- out_weight: bfloat16 [4096, 4096], P('tp'), may hold values from -0.09375 to 0.09375
Outputs:
- mixed: bfloat16 [6144, 4096], P('ctx', 'tp')
All inputs are finite; a program needn't handle non-finite values.
Results may differ from a plain program's by a relative error of at most 0.0072.
Values may be sent and summed in bfloat16 or wider, within the bound.
No kernel may reach another device: no remote copies, remote signals or barrier semaphores. Data moves between devices by JAX's collectives and lax.ppermute only.
A program may use at most 192 MiB of HBM per device.

v0:
```python
import jax
import jax.numpy as jnp
from jax import lax
from jax.sharding import PartitionSpec as P


def skewed(extended):
    group_size = extended.shape[0]
    width = extended.shape[1] // 2
    reverse = extended[:, ::-1]
    tiled = jnp.tile(reverse, (1, width))
    flat = tiled[:, width - 1 : width - 1 + width * (2 * width - 1)]
    return flat.reshape(group_size, width, 2 * width - 1)[:, :, :width]


def toeplitz_pair(filters):
    blank = jnp.zeros(filters.shape, jnp.float32)
    lower = skewed(jnp.concatenate([blank, filters], axis=1))
    upper = skewed(jnp.concatenate([filters, blank], axis=1))
    return (lower, upper)


def channel_filter(fields, short_weights, filters, skip_weights):
    group_size = fields.shape[1]
    length = fields.shape[2]
    short_count = short_weights.shape[2]
    medium_count = filters.shape[1]
    widened = jnp.pad(fields.astype(jnp.float32), ((0, 0), (0, 0), (short_count - 1, 0)))
    smoothed = jnp.zeros(fields.shape, jnp.float32)
    for lag_step in range(short_count):
        start_col = short_count - 1 - lag_step
        smoothed = (
            smoothed
            + short_weights[:, :, lag_step : lag_step + 1]
            * widened[:, :, start_col : start_col + length]
        )
    product = smoothed[1] * smoothed[2]
    blocks = product.reshape(group_size, -1, medium_count)
    earlier = jnp.concatenate(
        [jnp.zeros((group_size, 1, medium_count), jnp.float32), blocks[:, :-1]], axis=1
    )
    lower, upper = toeplitz_pair(filters)
    response = jnp.einsum("cbj,cij->cbi", blocks, lower, precision=lax.Precision.HIGHEST)
    response = response + jnp.einsum(
        "cbj,cij->cbi", earlier, upper, precision=lax.Precision.HIGHEST
    )
    response = response.reshape(group_size, -1)
    return (smoothed[0] * (response + skip_weights[:, None] * product)).astype(jnp.bfloat16)


def per_device(tokens, in_weight, short_taps, medium_taps, medium_decay, skip_gain, out_weight):
    row_count = tokens.shape[0]
    channel_count = in_weight.shape[2]
    ctx_count = lax.axis_size("ctx")
    group_size = channel_count // ctx_count
    medium_count = medium_taps.shape[1]
    features = jnp.einsum(
        "rd,dkc->rkc",
        tokens,
        lax.all_gather(in_weight, "ctx", axis=0, tiled=True),
        preferred_element_type=jnp.float32,
    ).astype(jnp.bfloat16)
    lag_values = lax.broadcasted_iota(jnp.float32, (1, medium_count), 1)
    filters = medium_taps * jnp.exp(-medium_decay[:, None] * lag_values)
    tilted = jnp.transpose(features, (1, 2, 0))
    spread = lax.all_to_all(tilted, "ctx", split_axis=1, concat_axis=2, tiled=True)
    offset = lax.axis_index("ctx") * group_size
    short_local = lax.dynamic_slice_in_dim(short_taps, offset, group_size, 1)
    filter_local = lax.dynamic_slice_in_dim(filters, offset, group_size, 0)
    skip_local = lax.dynamic_slice_in_dim(skip_gain, offset, group_size, 0)
    filtered = channel_filter(spread, short_local, filter_local, skip_local)
    filtered = filtered.reshape(group_size, ctx_count, row_count)
    returned = lax.all_to_all(filtered, "ctx", split_axis=1, concat_axis=0, tiled=True)
    gated = returned.reshape(channel_count, row_count)
    summed = lax.psum_scatter(
        lax.dot_general(
            out_weight, gated, (((0,), (0,)), ((), ())), preferred_element_type=jnp.float32
        ),
        "tp",
        scatter_dimension=0,
        tiled=True,
    )
    return jnp.transpose(summed).astype(jnp.bfloat16)


def solution(mesh):
    return jax.shard_map(
        per_device,
        mesh=mesh,
        in_specs=(
            P("ctx", None),
            P("ctx", None, "tp"),
            P(None, "tp", None),
            P("tp", None),
            P("tp"),
            P("tp"),
            P("tp", None),
        ),
        out_specs=P("ctx", "tp"),
        check_vma=False,
    )
```

profile of v0, /device:TPU:0, one launch (start us, length us, event | category | flops | bytes accessed | tf_op | source)
XLA Modules:
  0.0 935.4 jit_solution(1060447155559455234)
XLA Ops:
  6.5 0.0 all-gather.2.cloned.1.call-start
  6.5 4.7 copy.21
  11.2 0.0 all-gather.2.cloned.1.call-update
  11.3 483.3 %all-gather.2.cloned.1.call-done = bf16[4096,3,1024]{0,2,1:T(8,128)(2,1)} async-done(((bf16[512,3,1024]{0,2,1:T(8,128)(2,1)}), bf16[4096,3,1024]{0,2,1:T(8,128)(2,1)}) %all-gather.2.cloned.1.call-update) | async-done | bytes 25165840 | tf_op jit(solution)/shard_map/all_gather | solution.py:60
  494.6 24.9 %fusion.9 = bf16[3,1024,768]{2,1,0:T(8,128)(2,1)S(1)} fusion(bf16[4096,3,1024]{0,2,1:T(8,128)(2,1)} %all-gather.2.cloned.1.call-done, bf16[768,4096]{1,0:T(8,128)(2,1)} %param.7), kind=kOutput, calls=%fused_computation.14 | convolution fusion | flops 19329712128 | bytes 36175872 | tf_op jit(solution)/shard_map/rd,dkc->rkc/dot_general | solution.py:57
  519.5 6.6 copy.22
  526.1 0.0 copy-start.2
  526.1 4.9 all-to-all-start
  531.0 0.0 reduce-scatter.2.cloned.1.call-start
  531.0 0.0 copy-done.2
  531.1 0.8 dynamic_slice.11
  531.8 0.1 dynamic-slice.7
  531.9 1.0 constant_dynamic-slice_fusion.5
  533.0 0.9 dynamic-slice_multiply_fusion
  533.9 0.7 rev.6
  534.6 0.2 rev.7
  534.8 1.3 tile.20
  536.1 20.7 %copy.38 = f32[16,8,128,256]{3,1,2,0:T(8,128)S(1)} copy(f32[16,8,128,256]{3,2,1,0:T(8,128)S(1)} %bitcast.46) | data formatting | bytes 33554432
  556.8 7.5 slice.91
  564.2 28.9 %reshape.44 = f32[128,128,255]{2,1,0:T(8,128)} reshape(f32[128,32640]{1,0:T(8,128)} %slice.91) | data formatting | bytes 33423360 | tf_op jit(solution)/shard_map/reshape | solution.py:13
  593.1 1.3 tile.8
  594.5 20.7 %copy.37 = f32[16,8,128,256]{3,1,2,0:T(8,128)S(1)} copy(f32[16,8,128,256]{3,2,1,0:T(8,128)S(1)} %bitcast.47) | data formatting | bytes 33554432
  615.1 7.6 slice.88
  622.7 28.9 %reshape.43 = f32[128,128,255]{2,1,0:T(8,128)} reshape(f32[128,32640]{1,0:T(8,128)} %slice.88) | data formatting | bytes 33423360 | tf_op jit(solution)/shard_map/reshape | solution.py:13
  651.6 17.8 %all-to-all-done = bf16[3,1024,768]{2,0,1:T(4,128)(2,1)} async-done(((bf16[3,1024,768]{2,0,1:T(4,128)(2,1)}), bf16[3,1024,768]{2,0,1:T(4,128)(2,1)}, u32[]{:S(2)}, u32[]{:S(2)}) %all-to-all-start) | async-done | bytes 4718624 | tf_op jit(solution)/shard_map/all_to_all | solution.py:66
  669.4 3.4 copy.23
  672.8 4.8 convert_bitcast_fusion
  677.6 9.6 %copy.24 = f32[3,128,8,768]{1,3,2,0:T(8,128)} copy(f32[3,128,8,768]{3,1,2,0:T(8,128)} %convert_bitcast_fusion) | data formatting | bytes 18874368 | tf_op jit(solution)/shard_map/convert_element_type | solution.py:28
  687.2 30.6 %multiply_add_fusion = f32[3,128,6144]{1,2,0:T(8,128)} fusion(f32[3,128,6144]{1,2,0:T(8,128)} %bitcast.50, f32[3,128]{1,0:T(4,128)S(1)} %get-tuple-element.16, f32[3,128]{1,0:T(4,128)S(1)} %get-tuple-element.17, f32[3,128]{1,0:T(4,128)S(1)} %get-tuple-element.18, f32[3,128]{1,0:T(4,128)S(1)} %get-tuple-element.19, f32[3,128]{1,0:T(4,128)S(1)} %get-tuple-element.20, ...), kind=kLoop, calls=%fused_computation.1 | loop fusion | flops 30670848 | bytes 18885120 | tf_op jit(solution)/shard_map/add | solution.py:33
  717.8 5.9 slice_multiply_fusion
  723.7 3.5 copy.28
  727.2 2.4 copy.29
  729.5 2.3 copy.26
  731.9 0.0 copy-start
  731.9 16.0 %fusion = f32[128,48,128]{2,1,0:T(8,128)S(1)} fusion(f32[128,128,255]{2,1,0:T(8,128)} %reshape.44, f32[128,47,128]{2,1,0:T(8,128)} %bitcast.53), kind=kOutput, calls=%fused_computation.2 | convolution fusion | flops 1207959552 | bytes 14680064 | tf_op jit(solution)/shard_map/cbj,cij->cbi/dot_general | solution.py:44
  747.9 0.0 copy-done
  747.9 0.0 copy-start.1
  747.9 17.1 %fusion.12 = f32[128,48,128]{2,1,0:T(8,128)} fusion(f32[128,48,128]{2,1,0:T(8,128)S(1)} %fusion, f32[128,48,128]{2,1,0:T(8,128)S(1)} %copy-done, f32[128,128,255]{2,1,0:T(8,128)} %reshape.43), kind=kOutput, calls=%fused_computation.15 | convolution fusion | flops 1208745984 | bytes 17825792 | tf_op jit(solution)/shard_map/cbj,cij->cbi/dot_general | solution.py:43
  765.0 4.6 reshape.45
  769.6 0.0 copy-done.1
  769.7 4.1 fusion.7
  773.7 40.5 %all_to_all.24 = bf16[128,8,768]{2,0,1:T(8,128)(2,1)S(1)} all-to-all(bf16[128,8,768]{2,0,1:T(8,128)(2,1)S(1)} %fusion.7), channel_id=1, replica_groups=mesh['ctx'=8,'tp'=4] {'ctx'}, dimensions={1} | all-to-all | bytes 3145728 | tf_op jit(solution)/shard_map/all_to_all | solution.py:73
  814.3 12.5 %convolution_bitcast_fusion = f32[4096,768]{0,1:T(8,128)} fusion(bf16[1024,768]{1,0:T(8,128)(2,1)S(1)} %bitcast.56, bf16[1024,4096]{1,0:T(8,128)(2,1)} %param.13), kind=kOutput, calls=%fused_computation.6 | convolution fusion | flops 6442450944 | bytes 22544384 | tf_op jit(solution)/shard_map/dot_general | solution.py:76
  826.8 0.0 reduce-scatter.2.cloned.1.call-update
  826.8 98.2 %reduce-scatter.2.cloned.1.call-done = f32[1024,768]{0,1:T(8,128)} async-done(((f32[4096,768]{0,1:T(8,128)}), f32[1024,768]{0,1:T(8,128)}) %reduce-scatter.2.cloned.1.call-update) | async-done | bytes 3145744 | tf_op jit(solution)/shard_map/reduce_scatter | solution.py:75
  925.1 3.3 convert_bitcast_fusion.1
  (6 shorter events, 0.0 us)
Async XLA Ops:
  6.5 488.0 %all-gather.2.cloned.1.call-start = ((), (), s32[]{:S(2)}) async-start(), calls=%async_computation.3 | async-start | bytes 28311552 | tf_op jit(solution)/shard_map/all_gather | solution.py:60
  526.1 4.9 copy-start.2
  526.1 143.3 %all-to-all-start = ((bf16[3,1024,768]{2,0,1:T(4,128)(2,1)}), bf16[3,1024,768]{2,0,1:T(4,128)(2,1)}, u32[]{:S(2)}, u32[]{:S(2)}) async-start(bf16[3,1024,768]{2,0,1:T(4,128)(2,1)} %copy.22), calls=%async_computation | async-start | bytes 12582912 | tf_op jit(solution)/shard_map/all_to_all | solution.py:66
  531.0 394.1 %reduce-scatter.2.cloned.1.call-start = ((), (), s32[]{:S(2)}) async-start(), calls=%async_computation.4 | async-start | bytes 15728640 | tf_op jit(solution)/shard_map/reduce_scatter | solution.py:75
  731.9 16.0 %copy-start = (f32[128,48,128]{2,1,0:T(8,128)S(1)}, f32[128,48,128]{2,1,0:T(8,128)}, u32[]{:S(2)}) copy-start(f32[128,48,128]{2,1,0:T(8,128)} %copy.29) | copy-start | bytes 9437188
  747.9 21.7 %copy-start.1 = (f32[128,8,768]{2,0,1:T(8,128)S(1)}, f32[128,8,768]{2,0,1:T(8,128)}, u32[]{:S(2)}) copy-start(f32[128,8,768]{2,0,1:T(8,128)} %copy.28) | copy-start | bytes 9437188
Sparse Core Ops, SparseCore 0:
  11.4 483.1 all-gather.1
  827.0 98.0 reduce-scatter.1
where the time goes:
time: 943 us; the launch traced here: 935 us
  waiting for transfers between devices  599 us (64%)
  local copies, waits for them, and re-layouts  157 us (17%)
  matrix products  70.6 us (7%)
  other arithmetic  49.5 us (5%)
  blocking collectives  40.5 us (4%)
  between operations  13.8 us (1%)
    all_gather x1, waiting for transfers between devices, per_device(): lax.all_gather(in_weight, 'ctx', axis=0, tiled=True)  483 us
    reduce_scatter x1, waiting for transfers between devices, per_device(): lax.psum_scatter(lax.dot_general(out_weight, gated, (((0,), (0,)), ((), (...  98.2 us
    reshape x2, local copies, waits for them, and re-layouts, skewed(): return flat.reshape(group_size, width, 2 * width - 1)[:, :, :width]  57.8 us
    unnamed x13, local copies, waits for them, and re-layouts  46.1 us
    all_to_all x1, blocking collectives, per_device(): lax.all_to_all(filtered, 'ctx', split_axis=1, concat_axis=0, tiled=True)  40.5 us
    add x1, other arithmetic, channel_filter(): smoothed + short_weights[:, :, lag_step:lag_step + 1] * widened[:, :, sta...  30.6 us
    dot_general x1, matrix products, per_device(): jnp.einsum('rd,dkc->rkc', tokens, lax.all_gather(in_weight, 'ctx', axis=0...  24.9 us
  transfers between devices with their start and end apart: 3, of which 3 were waited for; matrix products, arithmetic and copies ran while one was open for 13% of the time, Pallas kernels for 0%

commit v1 on v0

--- a/solution.py
+++ b/solution.py
@@ -2,6 +2,39 @@
 import jax.numpy as jnp
 from jax import lax
 from jax.sharding import PartitionSpec as P
+
+
+def _put_edges(xs, along_dim):
+    v1, front, oldest = (lax.axis_size("ctx"), lax.axis_index("ctx"), xs.shape[along_dim])
+    cards = []
+    j0 = 0
+    while j0 < v1:
+        cards.append((j0, (j0 + 1) % v1))
+        j0 += 1
+    inbox = []
+    j0 = 0
+    while j0 < v1:
+        inbox.append((j0, (j0 - 1) % v1))
+        j0 += 1
+    outcome_arr = jnp.zeros(
+        (*xs.shape[:along_dim], v1 * oldest, *xs.shape[along_dim + 1 :]), xs.dtype
+    )
+    outcome_arr = lax.dynamic_update_slice_in_dim(outcome_arr, xs, front * oldest, axis=along_dim)
+    before = now = xs
+    local_now = v1 // 2
+    idx = 1
+    while idx < local_now + 1:
+        before = lax.ppermute(before, "ctx", cards)
+        outcome_arr = lax.dynamic_update_slice_in_dim(
+            outcome_arr, before, (front - idx) % v1 * oldest, axis=along_dim
+        )
+        if idx < v1 - local_now:
+            now = lax.ppermute(now, "ctx", inbox)
+            outcome_arr = lax.dynamic_update_slice_in_dim(
+                outcome_arr, now, (front + idx) % v1 * oldest, axis=along_dim
+            )
+        idx += 1
+    return outcome_arr
 
 
 def skewed(extended):
@@ -57,7 +90,7 @@
     features = jnp.einsum(
         "rd,dkc->rkc",
         tokens,
-        lax.all_gather(in_weight, "ctx", axis=0, tiled=True),
+        _put_edges(in_weight, along_dim=0),
         preferred_element_type=jnp.float32,
     ).astype(jnp.bfloat16)
     lag_values = lax.broadcasted_iota(jnp.float32, (1, medium_count), 1)

time: 943 us -> 953 us (1.011)
  waiting for transfers between devices: 599 us -> 521 us
  local copies, waits for them, and re-layouts: 157 us -> 213 us
  starting transfers between devices: 4.91 us -> 24.5 us
  matrix products: 70.6 us -> 82.1 us
    all_gather x1 -> x0, waiting for transfers between devices: 483 us -> none  [per_device(): lax.all_gather(in_weight, 'ctx', axis=0, tiled=True)]
    ppermute x0 -> x7, waiting for transfers between devices: none -> 408 us  [the longest x4 408 us: _put_edges(): before = lax.ppermute(before, 'ctx', cards)]
    ppermute x0 -> x7, local copies, waits for them, and re-layouts: none -> 26.7 us  [the longest x4 15.7 us: _put_edges(): before = lax.ppermute(before, 'ctx', cards)]
    ppermute x0 -> x7, starting transfers between devices: none -> 19.6 us  [the longest x4 10.4 us: _put_edges(): before = lax.ppermute(before, 'ctx', cards)]
    dynamic_update_slice x0 -> x8, local copies, waits for them, and re-layouts: none -> 19.2 us  [the longest x4 11.5 us: _put_edges(): lax.dynamic_update_slice_in_dim(outcome_arr, before, (front - idx) % v1 *...]
    dot_general x1, matrix products: 24.9 us -> 36.5 us  [per_device(): jnp.einsum('rd,dkc->rkc', tokens, _put_edges(in_weight, along_dim=0), pre...]
    unnamed x13 -> x21, local copies, waits for them, and re-layouts: 46.1 us -> 47.3 us
  transfers between devices with their start and end apart: 3 -> 9, of which waited for: 3 -> 6; matrix products, arithmetic and copies ran while one was open for 13% -> 18% of each run, Pallas kernels for 0% -> 0%
where the time goes in v1:
time: 953 us; the launch traced here: 945 us
  waiting for transfers between devices  521 us (55%)
  local copies, waits for them, and re-layouts  213 us (22%)
  matrix products  82.1 us (9%)
  other arithmetic  49.4 us (5%)
  blocking collectives  40.6 us (4%)
  starting transfers between devices  24.5 us (3%)
  between operations  14.2 us (1%)
    ppermute x4, waiting for transfers between devices, _put_edges(): before = lax.ppermute(before, 'ctx', cards)  408 us
    reduce_scatter x1, waiting for transfers between devices, per_device(): lax.psum_scatter(lax.dot_general(out_weight, gated, (((0,), (0,)), ((), (...  98.3 us
    reshape x2, local copies, waits for them, and re-layouts, skewed(): return flat.reshape(group_size, width, 2 * width - 1)[:, :, :width]  57.8 us
    unnamed x21, local copies, waits for them, and re-layouts  47.3 us
    all_to_all x1, blocking collectives, per_device(): lax.all_to_all(filtered, 'ctx', split_axis=1, concat_axis=0, tiled=True)  40.6 us
    dot_general x1, matrix products, per_device(): jnp.einsum('rd,dkc->rkc', tokens, _put_edges(in_weight, along_dim=0), pre...  36.5 us
    add x1, other arithmetic, channel_filter(): smoothed + short_weights[:, :, lag_step:lag_step + 1] * widened[:, :, sta...  30.4 us
  transfers between devices with their start and end apart: 9, of which 6 were waited for; matrix products, arithmetic and copies ran while one was open for 18% of the time, Pallas kernels for 0%

profile of v1, /device:TPU:0, one launch (start us, length us, event | category | flops | bytes accessed | tf_op | source)
XLA Modules:
  0.0 945.0 jit_solution(18441965568147669737)
XLA Ops:
  6.5 3.0 collective-permute-start
  9.5 3.0 collective-permute-start.1
  12.5 132.0 %collective-permute-done = bf16[512,3,1024]{2,0,1:T(8,128)(2,1)S(1)} collective-permute-done((bf16[512,3,1024]{2,0,1:T(8,128)(2,1)}, bf16[512,3,1024]{2,0,1:T(8,128)(2,1)S(1)}, u32[]{:S(2)}, u32[]{:S(2)}) %collective-permute-start) | collective-permute-done | bytes 3145760 | tf_op jit(solution)/shard_map/ppermute | solution.py:27
  144.6 2.4 collective-permute-start.2
  147.0 3.1 collective-permute-start.3
  150.1 130.8 %collective-permute-done.2 = bf16[512,3,1024]{2,0,1:T(8,128)(2,1)S(1)} collective-permute-done((bf16[512,3,1024]{2,0,1:T(8,128)(2,1)S(1)}, bf16[512,3,1024]{2,0,1:T(8,128)(2,1)S(1)}, u32[]{:S(2)}, u32[]{:S(2)}) %collective-permute-start.2) | collective-permute-done | bytes 3145760 | tf_op jit(solution)/shard_map/ppermute | solution.py:27
  280.9 1.6 copy-done.3
  282.5 2.5 collective-permute-start.4
  285.0 3.0 collective-permute-start.5
  288.0 130.1 %collective-permute-done.4 = bf16[512,3,1024]{2,0,1:T(8,128)(2,1)} collective-permute-done((bf16[512,3,1024]{2,0,1:T(8,128)(2,1)S(1)}, bf16[512,3,1024]{2,0,1:T(8,128)(2,1)}, u32[]{:S(2)}, u32[]{:S(2)}) %collective-permute-start.4) | collective-permute-done | bytes 3145760 | tf_op jit(solution)/shard_map/ppermute | solution.py:27
  418.1 2.6 collective-permute-start.6
  420.7 3.2 copy.42
  424.0 8.5 broadcast_in_dim.2
  432.5 1.9 constant_dynamic-update-slice_fusion.7
  434.5 4.6 copy.43
  439.1 3.2 copy.44
  442.3 3.8 constant_dynamic-update-slice_fusion.6
  446.1 1.9 constant_dynamic-update-slice_fusion.5
  448.1 4.7 copy.45
  452.7 3.2 copy.46
  455.9 3.8 constant_dynamic-update-slice_fusion.4
  459.7 1.9 constant_dynamic-update-slice_fusion.3
  461.7 3.2 copy.47
  464.9 4.7 copy.48
  469.5 1.9 constant_dynamic-update-slice_fusion.2
  471.5 1.1 copy-done.1
  472.5 2.0 constant_dynamic-update-slice_fusion.1
  474.5 15.2 %collective-permute-done.6 = bf16[512,3,1024]{2,0,1:T(8,128)(2,1)} collective-permute-done((bf16[512,3,1024]{2,0,1:T(8,128)(2,1)}, bf16[512,3,1024]{2,0,1:T(8,128)(2,1)}, u32[]{:S(2)}, u32[]{:S(2)}) %collective-permute-start.6) | collective-permute-done | bytes 3145760 | tf_op jit(solution)/shard_map/ppermute | solution.py:27
  489.7 3.2 copy.49
  492.9 1.9 constant_dynamic-update-slice_fusion
  494.8 36.5 %fusion.9 = bf16[3,1024,768]{2,1,0:T(8,128)(2,1)S(1)} fusion(bf16[4096,3,1024]{0,2,1:T(8,128)(2,1)} %constant_dynamic-update-slice_fusion, bf16[768,4096]{1,0:T(8,128)(2,1)} %param.7), kind=kOutput, calls=%fused_computation.14 | convolution fusion | flops 19329712128 | bytes 36175872 | tf_op jit(solution)/shard_map/rd,dkc->rkc/dot_general | solution.py:90
  531.4 6.6 copy.50
  538.0 4.9 all-to-all-start
  542.9 1.3 constant_dynamic-slice_fusion.5
  544.2 0.1 dynamic-slice.7
  544.3 0.9 dynamic-slice_multiply_fusion
  545.3 0.2 rev.7
  545.5 1.3 tile.20
  546.8 20.7 %copy.66 = f32[16,8,128,256]{3,1,2,0:T(8,128)S(1)} copy(f32[16,8,128,256]{3,2,1,0:T(8,128)S(1)} %bitcast.46) | data formatting | bytes 33554432
  567.5 7.5 slice.91
  575.0 28.9 %reshape.44 = f32[128,128,255]{2,1,0:T(8,128)} reshape(f32[128,32640]{1,0:T(8,128)} %slice.91) | data formatting | bytes 33423360 | tf_op jit(solution)/shard_map/reshape | solution.py:46
  603.9 0.2 rev.6
  604.0 1.3 tile.8
  605.4 20.7 %copy.65 = f32[16,8,128,256]{3,1,2,0:T(8,128)S(1)} copy(f32[16,8,128,256]{3,2,1,0:T(8,128)S(1)} %bitcast.47) | data formatting | bytes 33554432
  626.1 7.6 slice.88
  633.6 28.9 %reshape.43 = f32[128,128,255]{2,1,0:T(8,128)} reshape(f32[128,32640]{1,0:T(8,128)} %slice.88) | data formatting | bytes 33423360 | tf_op jit(solution)/shard_map/reshape | solution.py:46
  662.6 0.8 dynamic_slice.11
  663.3 15.0 %all-to-all-done = bf16[3,1024,768]{2,0,1:T(4,128)(2,1)} async-done(((bf16[3,1024,768]{2,0,1:T(4,128)(2,1)}), bf16[3,1024,768]{2,0,1:T(4,128)(2,1)}, u32[]{:S(2)}, u32[]{:S(2)}) %all-to-all-start) | async-done | bytes 4718624 | tf_op jit(solution)/shard_map/all_to_all | solution.py:99
  678.4 3.4 copy.51
  681.8 4.8 convert_bitcast_fusion
  686.6 9.8 %copy.52 = f32[3,128,8,768]{1,3,2,0:T(8,128)} copy(f32[3,128,8,768]{3,1,2,0:T(8,128)} %convert_bitcast_fusion) | data formatting | bytes 18874368 | tf_op jit(solution)/shard_map/convert_element_type | solution.py:61
  696.3 30.4 %multiply_add_fusion = f32[3,128,6144]{1,2,0:T(8,128)} fusion(f32[3,128,6144]{1,2,0:T(8,128)} %bitcast.50, f32[3,128]{1,0:T(4,128)S(1)} %get-tuple-element.16, f32[3,128]{1,0:T(4,128)S(1)} %get-tuple-element.17, f32[3,128]{1,0:T(4,128)S(1)} %get-tuple-element.18, f32[3,128]{1,0:T(4,128)S(1)} %get-tuple-element.19, f32[3,128]{1,0:T(4,128)S(1)} %get-tuple-element.20, ...), kind=kLoop, calls=%fused_computation.1 | loop fusion | flops 30670848 | bytes 18885120 | tf_op jit(solution)/shard_map/add | solution.py:66
  726.8 5.9 slice_multiply_fusion
  732.7 2.4 copy.57
  735.1 16.0 %fusion = f32[128,48,128]{2,1,0:T(8,128)S(1)} fusion(f32[128,128,255]{2,1,0:T(8,128)} %reshape.44, f32[128,47,128]{2,1,0:T(8,128)} %bitcast.53), kind=kOutput, calls=%fused_computation.2 | convolution fusion | flops 1207959552 | bytes 14680064 | tf_op jit(solution)/shard_map/cbj,cij->cbi/dot_general | solution.py:77
  751.1 17.0 %fusion.12 = f32[128,48,128]{2,1,0:T(8,128)} fusion(f32[128,48,128]{2,1,0:T(8,128)S(1)} %fusion, f32[128,48,128]{2,1,0:T(8,128)S(1)} %copy-done, f32[128,128,255]{2,1,0:T(8,128)} %reshape.43), kind=kOutput, calls=%fused_computation.15 | convolution fusion | flops 1208745984 | bytes 17825792 | tf_op jit(solution)/shard_map/cbj,cij->cbi/dot_general | solution.py:76
  768.1 4.6 reshape.45
  772.8 2.4 copy.54
  775.2 3.7 copy.56
  778.9 4.1 fusion.7
  783.0 40.6 %all_to_all.24 = bf16[128,8,768]{2,0,1:T(8,128)(2,1)S(1)} all-to-all(bf16[128,8,768]{2,0,1:T(8,128)(2,1)S(1)} %fusion.7), channel_id=1, replica_groups=mesh['ctx'=8,'tp'=4] {'ctx'}, dimensions={1} | all-to-all | bytes 3145728 | tf_op jit(solution)/shard_map/all_to_all | solution.py:106
  823.6 12.5 %convolution_bitcast_fusion = f32[4096,768]{0,1:T(8,128)} fusion(bf16[1024,768]{1,0:T(8,128)(2,1)S(1)} %bitcast.56, bf16[1024,4096]{1,0:T(8,128)(2,1)} %param.13), kind=kOutput, calls=%fused_computation.6 | convolution fusion | flops 6442450944 | bytes 22544384 | tf_op jit(solution)/shard_map/dot_general | solution.py:109
  836.1 98.3 %reduce-scatter.2.cloned.1.call-done = f32[1024,768]{0,1:T(8,128)} async-done(((f32[4096,768]{0,1:T(8,128)}), f32[1024,768]{0,1:T(8,128)}) %reduce-scatter.2.cloned.1.call-update) | async-done | bytes 3145744 | tf_op jit(solution)/shard_map/reduce_scatter | solution.py:108
  934.4 3.3 convert_bitcast_fusion.1
  (23 shorter events, 0.1 us)
Async XLA Ops:
  6.5 138.1 %collective-permute-start = (bf16[512,3,1024]{2,0,1:T(8,128)(2,1)}, bf16[512,3,1024]{2,0,1:T(8,128)(2,1)S(1)}, u32[]{:S(2)}, u32[]{:S(2)}) collective-permute-start(bf16[512,3,1024]{2,0,1:T(8,128)(2,1)} %param.8), channel_id=1, source_target_pairs={{0,4},{4,8},{8,12},{12,16},{16,20},{20,24},{24,28},{28,0},{1,5},{5... | collective-permute-start | bytes 9437192 | tf_op jit(solution)/shard_map/ppermute | solution.py:27
  9.5 137.5 %collective-permute-start.1 = (bf16[512,3,1024]{2,0,1:T(8,128)(2,1)}, bf16[512,3,1024]{2,0,1:T(8,128)(2,1)S(1)}, u32[]{:S(2)}, u32[]{:S(2)}) collective-permute-start(bf16[512,3,1024]{2,0,1:T(8,128)(2,1)} %param.8), channel_id=1, source_target_pairs={{0,28},{4,0},{8,4},{12,8},{16,12},{20,16},{24,20},{28,24},{1,29},{... | collective-permute-start | bytes 9437192 | tf_op jit(solution)/shard_map/ppermute | solution.py:32
  144.6 273.5 %copy-start.4 = (bf16[512,3,1024]{2,0,1:T(8,128)(2,1)}, bf16[512,3,1024]{2,0,1:T(8,128)(2,1)S(1)}, u32[]{:S(2)}) copy-start(bf16[512,3,1024]{2,0,1:T(8,128)(2,1)S(1)} %collective-permute-done) | copy-start | bytes 9437188
  144.6 136.3 %collective-permute-start.2 = (bf16[512,3,1024]{2,0,1:T(8,128)(2,1)S(1)}, bf16[512,3,1024]{2,0,1:T(8,128)(2,1)S(1)}, u32[]{:S(2)}, u32[]{:S(2)}) collective-permute-start(bf16[512,3,1024]{2,0,1:T(8,128)(2,1)S(1)} %collective-permute-done), channel_id=1, source_target_pairs={{0,4},{4,8},{8,12},{12,16},{16,20},{20,24},{24,28},{28,0},{1,5},{5... | collective-permute-start | bytes 9437192 | tf_op jit(solution)/shard_map/ppermute | solution.py:27
  147.0 273.7 %copy-start.5 = (bf16[512,3,1024]{2,0,1:T(8,128)(2,1)}, bf16[512,3,1024]{2,0,1:T(8,128)(2,1)S(1)}, u32[]{:S(2)}) copy-start(bf16[512,3,1024]{2,0,1:T(8,128)(2,1)S(1)} %collective-permute-done.1) | copy-start | bytes 9437188
  147.0 138.0 %collective-permute-start.3 = (bf16[512,3,1024]{2,0,1:T(8,128)(2,1)S(1)}, bf16[512,3,1024]{2,0,1:T(8,128)(2,1)}, u32[]{:S(2)}, u32[]{:S(2)}) collective-permute-start(bf16[512,3,1024]{2,0,1:T(8,128)(2,1)S(1)} %collective-permute-done.1), channel_id=1, source_target_pairs={{0,28},{4,0},{8,4},{12,8},{16,12},{20,16},{24,20},{28,24},{1,29},{... | collective-permute-start | bytes 9437192 | tf_op jit(solution)/shard_map/ppermute | solution.py:32
  280.9 1.6 copy-start.3
  282.5 135.6 %collective-permute-start.4 = (bf16[512,3,1024]{2,0,1:T(8,128)(2,1)S(1)}, bf16[512,3,1024]{2,0,1:T(8,128)(2,1)}, u32[]{:S(2)}, u32[]{:S(2)}) collective-permute-start(bf16[512,3,1024]{2,0,1:T(8,128)(2,1)S(1)} %collective-permute-done.2), channel_id=1, source_target_pairs={{0,4},{4,8},{8,12},{12,16},{16,20},{20,24},{24,28},{28,0},{1,5},{5... | collective-permute-start | bytes 9437192 | tf_op jit(solution)/shard_map/ppermute | solution.py:27
  285.0 179.9 %collective-permute-start.5 = (bf16[512,3,1024]{2,0,1:T(8,128)(2,1)}, bf16[512,3,1024]{2,0,1:T(8,128)(2,1)}, u32[]{:S(2)}, u32[]{:S(2)}) collective-permute-start(bf16[512,3,1024]{2,0,1:T(8,128)(2,1)} %collective-permute-done.3), channel_id=1, source_target_pairs={{0,28},{4,0},{8,4},{12,8},{16,12},{20,16},{24,20},{28,24},{1,29},{... | collective-permute-start | bytes 9437192 | tf_op jit(solution)/shard_map/ppermute | solution.py:32
  418.1 71.6 %collective-permute-start.6 = (bf16[512,3,1024]{2,0,1:T(8,128)(2,1)}, bf16[512,3,1024]{2,0,1:T(8,128)(2,1)}, u32[]{:S(2)}, u32[]{:S(2)}) collective-permute-start(bf16[512,3,1024]{2,0,1:T(8,128)(2,1)} %collective-permute-done.4), channel_id=1, source_target_pairs={{0,4},{4,8},{8,12},{12,16},{16,20},{20,24},{24,28},{28,0},{1,5},{5... | collective-permute-start | bytes 9437192 | tf_op jit(solution)/shard_map/ppermute | solution.py:27
  469.5 3.0 copy-start.1
  538.0 6.2 copy-start.6
  538.0 140.4 %all-to-all-start = ((bf16[3,1024,768]{2,0,1:T(4,128)(2,1)}), bf16[3,1024,768]{2,0,1:T(4,128)(2,1)}, u32[]{:S(2)}, u32[]{:S(2)}) async-start(bf16[3,1024,768]{2,0,1:T(4,128)(2,1)} %copy.50), calls=%async_computation | async-start | bytes 12582912 | tf_op jit(solution)/shard_map/all_to_all | solution.py:99
  542.9 391.5 %reduce-scatter.2.cloned.1.call-start = ((), (), s32[]{:S(2)}) async-start(), calls=%async_computation.3 | async-start | bytes 15728640 | tf_op jit(solution)/shard_map/reduce_scatter | solution.py:108
  735.1 16.0 %copy-start = (f32[128,48,128]{2,1,0:T(8,128)S(1)}, f32[128,48,128]{2,1,0:T(8,128)}, u32[]{:S(2)}) copy-start(f32[128,48,128]{2,1,0:T(8,128)} %copy.57) | copy-start | bytes 9437188
  775.2 3.7 copy-start.2
Sparse Core Ops, SparseCore 0:
  836.2 98.1 reduce-scatter.1
